TPU v7x, 32 devices: a whole 2x2x4 slice. The times are simulated.
32 devices in a mesh: section: 4 (over x, core), expert: 8 (over z, y).
Axes of the slice: x: 2, y: 2, z: 4, core: 2. Of those that a mesh axis runs over, the one named last changes fastest.
Arguments:
- layer_inputs: bfloat16 [4, 8, 128, 2048], P('section', None, 'expert'), may hold values from -6 to 6
- top_grad: bfloat16 [8, 128, 2048], P('section', 'expert'), may hold values from -6 to 6
- expert_ids: int32 [4, 8, 128, 4], P('section', None, 'expert'), may hold values from 0 to 7, all different within a row; in each aligned block of 16 rows (0 to 15, 16 to 31, ..., all dimensions but the last counted through in order) at most 9 rows name the same one
- router: bfloat16 [4, 2048, 8], P('section'), may hold values from -0.125 to 0.125
- norm_gain: bfloat16 [4, 2048], P('section'), may hold values from 0.099609375 to 1.8984375
- w_gate: bfloat16 [4, 8, 2048, 1024], P('section', 'expert'), may hold values from -0.125 to 0.125
- w_up: bfloat16 [4, 8, 2048, 1024], P('section', 'expert'), may hold values from -0.125 to 0.125
- w_down: bfloat16 [4, 8, 1024, 2048], P('section', 'expert'), may hold values from -0.1875 to 0.1875
Outputs:
- input_grads: bfloat16 [4, 8, 128, 2048], P('section', None, 'expert')
Inputs may be any that keep to these rules, and one draw needn't show every extreme that they name: `expert_ids`: each token names 4 different experts. Among the 16 tokens of one device in one micro-batch of one layer, no expert is named by more than 9 of them, and in some of these blocks one expert is named by exactly 9.
All inputs are finite; a program needn't handle non-finite values.
Results may differ from a plain program's by a relative error of at most 0.015.
Values may be sent and summed in bfloat16 or wider, within the bound.
No kernel may reach another device: no remote copies, remote signals or barrier semaphores. Data moves between devices by JAX's collectives and lax.ppermute only.
A program may use at most 128 MiB of HBM per device.

v0:
```python
import jax
import jax.numpy as jnp
from jax import lax
from jax.sharding import PartitionSpec as P


def shifted(shard, axis, by):
    devices = lax.axis_size(axis)
    pairs = [(i, i + by) for i in range(devices) if 0 <= i + by < devices]
    return lax.ppermute(shard, axis, pairs)


def prepare(x_rows, gain):
    x_float = x_rows.astype(jnp.float32)
    inverse = lax.rsqrt(jnp.mean(x_float * x_float, axis=-1, keepdims=True) + 1e-05)
    normed = (x_float * inverse * gain).astype(jnp.bfloat16)
    return (x_float, inverse, normed)


def expert_rows(normed_rows, grad_rows, gate_w, up_w, down_w):
    gate = jnp.dot(normed_rows, gate_w, preferred_element_type=jnp.float32)
    up_rows = jnp.dot(normed_rows, up_w, preferred_element_type=jnp.float32)
    squash = jax.nn.sigmoid(gate)
    active = gate * squash
    hidden = (active * up_rows).astype(jnp.bfloat16)
    output = jnp.dot(hidden, down_w, preferred_element_type=jnp.float32)
    dprob = jnp.sum(output * grad_rows.astype(jnp.float32), axis=-1)
    dhidden = lax.dot_general(
        grad_rows, down_w, (((1,), (1,)), ((), ())), preferred_element_type=jnp.float32
    )
    dgate = (dhidden * up_rows * squash * (1.0 + gate * (1.0 - squash))).astype(jnp.bfloat16)
    dup = (dhidden * active).astype(jnp.bfloat16)
    returned = lax.dot_general(
        dgate, gate_w, (((1,), (1,)), ((), ())), preferred_element_type=jnp.float32
    )
    returned = returned + lax.dot_general(
        dup, up_w, (((1,), (1,)), ((), ())), preferred_element_type=jnp.float32
    )
    return (returned.astype(jnp.bfloat16), dprob)


def finish(x_float, inverse, normed, gain, router_layer, ids, grad_in, pair_back, pair_prob):
    logits = jnp.dot(normed, router_layer, preferred_element_type=jnp.float32)
    raised = jnp.exp(logits)
    probs = raised / jnp.sum(raised, axis=-1, keepdims=True)
    choose = (ids[..., None] == jnp.arange(router_layer.shape[1], dtype=jnp.int32)).astype(
        jnp.float32
    )
    picked = jnp.sum(probs[..., None, :] * choose, axis=-1)
    dfull = jnp.sum(pair_prob[..., None] * choose, axis=-2)
    dlogit = probs * (dfull - jnp.sum(probs * dfull, axis=-1, keepdims=True))
    router_term = jnp.dot(
        dlogit, router_layer.astype(jnp.float32).T, precision=lax.Precision.HIGHEST
    )
    dnormed = jnp.sum(picked[..., None] * pair_back, axis=-2) + router_term
    scaled = gain * dnormed
    inner = jnp.mean(x_float * scaled, axis=-1, keepdims=True)
    result = (
        grad_in.astype(jnp.float32)
        + inverse * scaled
        - x_float * inverse * inverse * inverse * inner
    )
    return result.astype(jnp.bfloat16)


def selection(ids, experts, capacity):
    pair_ids = ids.reshape(-1)
    onehot = (pair_ids[:, None] == jnp.arange(experts, dtype=jnp.int32)[None, :]).astype(jnp.int32)
    ranks = jnp.sum(onehot * (jnp.cumsum(onehot, axis=0) - 1), axis=1)
    target = pair_ids * capacity + ranks
    return (target[:, None] == jnp.arange(experts * capacity, dtype=jnp.int32)[None, :]).astype(
        jnp.bfloat16
    )


def pack_rows(select, rows, per_token):
    repeated = jnp.repeat(rows, per_token, axis=0)
    packed = lax.dot_general(
        select, repeated, (((0,), (0,)), ((), ())), preferred_element_type=jnp.float32
    )
    return packed.astype(jnp.bfloat16)


def pick_micro(values, index):
    return lax.dynamic_index_in_dim(values, index, 0, False)


def shards(layer_inputs, top_grad, expert_ids, router, norm_gain, w_gate, w_up, w_down):
    segments = lax.axis_size("section")
    experts = lax.axis_size("expert")
    segment_index = lax.axis_index("section")
    micro = layer_inputs.shape[1]
    tok_rows = layer_inputs.shape[2]
    width = layer_inputs.shape[3]
    per_token = expert_ids.shape[3]
    capacity = min(tok_rows, per_token * tok_rows // experts + max(1, tok_rows // 16))
    slots = experts * capacity
    gain = norm_gain[0].astype(jnp.float32)
    router_layer = router[0]
    gate_layer = w_gate[0, 0]
    up_layer = w_up[0, 0]
    down_layer = w_down[0, 0]
    ids_layer = expert_ids[0]
    x_layer = layer_inputs[0]
    top_full = lax.all_gather(top_grad, "section", axis=0, tiled=True)

    def advance(step, carry):
        previous, collected = carry
        arrived = shifted(previous, "section", -1)
        position = step - (segments - 1 - segment_index)
        working = jnp.logical_and(position >= 0, position < micro)
        chosen = jnp.clip(position, 0, micro - 1)
        grad_in = jnp.where(segment_index == segments - 1, pick_micro(top_full, chosen), arrived)
        ids_now = pick_micro(ids_layer, chosen)
        select = selection(ids_now, experts, capacity)
        x_float, inverse, normed = prepare(pick_micro(x_layer, chosen), gain)
        sent_normed = pack_rows(select, normed, per_token).reshape(experts, capacity, width)
        sent_grad = pack_rows(select, grad_in, per_token).reshape(experts, capacity, width)
        got_normed, got_grad = (
            lax.all_to_all(sent_normed, "expert", split_axis=0, concat_axis=0, tiled=True),
            lax.all_to_all(sent_grad, "expert", split_axis=0, concat_axis=0, tiled=True),
        )
        rows_normed = got_normed.reshape(slots, width)
        rows_grad = got_grad.reshape(slots, width)

        def run_expert(operands):
            return expert_rows(operands[0], operands[1], gate_layer, up_layer, down_layer)

        def skip_expert(operands):
            return (jnp.zeros((slots, width), jnp.bfloat16), jnp.zeros((slots,), jnp.float32))

        returned, dprob = lax.cond(working, run_expert, skip_expert, (rows_normed, rows_grad))
        back_home, prob_home = (
            lax.all_to_all(
                returned.reshape(experts, capacity, width),
                "expert",
                split_axis=0,
                concat_axis=0,
                tiled=True,
            ),
            lax.all_to_all(
                dprob.reshape(experts, capacity).astype(jnp.bfloat16),
                "expert",
                split_axis=0,
                concat_axis=0,
                tiled=True,
            ).astype(jnp.float32),
        )
        pair_back = lax.dot_general(
            select,
            back_home.reshape(slots, width),
            (((1,), (0,)), ((), ())),
            preferred_element_type=jnp.float32,
        )
        pair_back = pair_back.reshape(tok_rows, per_token, width)
        pair_prob = jnp.dot(
            select.astype(jnp.float32), prob_home.reshape(slots), precision=lax.Precision.HIGHEST
        )
        pair_prob = pair_prob.reshape(tok_rows, per_token)
        result = finish(
            x_float, inverse, normed, gain, router_layer, ids_now, grad_in, pair_back, pair_prob
        )
        retained = pick_micro(collected, chosen)
        collected = lax.dynamic_update_index_in_dim(
            collected, jnp.where(working, result, retained), chosen, 0
        )
        return (result, collected)

    start = (
        jnp.zeros((tok_rows, width), jnp.bfloat16),
        jnp.zeros((micro, tok_rows, width), jnp.bfloat16),
    )
    final_grad, collected = lax.fori_loop(0, micro + segments - 1, advance, start)
    return collected.reshape(1, micro, tok_rows, width)


def solution(mesh):
    placed = (
        P("section", None, "expert", None),
        P("section", "expert", None),
        P("section", None, "expert", None),
        P("section", None, None),
        P("section", None),
        P("section", "expert", None, None),
        P("section", "expert", None, None),
        P("section", "expert", None, None),
    )
    return jax.shard_map(
        shards,
        mesh=mesh,
        in_specs=placed,
        out_specs=P("section", None, "expert", None),
        check_vma=False,
    )
```

profile of v0, /device:TPU:2, one launch (start us, length us, event | category | flops | bytes accessed | tf_op | source)
XLA Modules:
  0.0 932.1 jit_solution(10642153080023947241)
XLA Ops:
  9.2 922.1 %while.18 = (s32[]{:T(128)}, bf16[16,2048]{1,0:T(8,128)(2,1)S(1)}, bf16[8,16,2048]{2,1,0:T(8,128)(2,1)S(1)}, pred[]{:T(512)}, s32[]{:T(128)}, /*index=5*/bf16[8,...) while((s32[]{:T(128)}, bf16[16,2048]{1,0:T(8,128)(2,1)S(1)}, ...), condition=%wide.region_13.14_spmd.clone, body=%wide.region_0.13_spmd.clone.sunk | while | flops 1876001664 | bytes 93928576 | solution.py:173
  40.5 14.4 %all-to-all-done = bf16[8,9,2048]{2,1,0:T(8,128)(2,1)S(1)} async-done(((bf16[8,9,2048]{2,1,0:T(8,128)(2,1)}), bf16[8,9,2048]{2,1,0:T(8,128)(2,1)S(1)}, u32[]{:S(2)}, u32[]{:S(2)}) %all-to-all-start) | async-done | bytes 294944 | tf_op jit(solution)/shard_map/while/body/eval_jaxpr/all_to_all | solution.py:121
  120.1 14.1 %conditional.3 = (bf16[72,2048]{1,0:T(8,128)(2,1)S(1)}, bf16[72]{0:T(256)(128)(2,1)S(1)}) conditional(s32[]{:T(128)} %convert_element_type.180, () %tuple.64, (bf16[8,9,2048]{2,1,0:T(8,128)(2,1)S(1)}, bf16[1024,2048]{1,0:T(8,128)(2,1)}, bf16[8,9,2048]{2,1,0:T(8,128)(2,1)S(1)}, bf16[2048,1024]{1,0:T(8,128)(2,1)}, bf16[2048,1024]{1,0:T(8,128)(2,1)}) %tuple.65), branch_computations={%region_6.6_spmd, %region_7.8_spmd} | conditional | flops 1814298624 | bytes 82280696 | solution.py:132
  151.3 14.9 %all-to-all-done.2 = bf16[8,9,2048]{2,1,0:T(8,128)(2,1)S(1)} async-done(((bf16[8,9,2048]{2,1,0:T(8,128)(2,1)}), bf16[8,9,2048]{2,1,0:T(8,128)(2,1)S(1)}, u32[]{:S(2)}, u32[]{:S(2)}) %all-to-all-start.2) | async-done | bytes 294944 | tf_op jit(solution)/shard_map/while/body/eval_jaxpr/all_to_all | solution.py:134
  180.9 13.7 %all-to-all-done.1 = bf16[8,9,2048]{2,1,0:T(8,128)(2,1)S(1)} async-done(((bf16[8,9,2048]{2,1,0:T(8,128)(2,1)}), bf16[8,9,2048]{2,1,0:T(8,128)(2,1)S(1)}, u32[]{:S(2)}, u32[]{:S(2)}) %all-to-all-start.1) | async-done | bytes 294944 | tf_op jit(solution)/shard_map/while/body/eval_jaxpr/all_to_all | solution.py:120
  198.4 14.5 %all-to-all-done = bf16[8,9,2048]{2,1,0:T(8,128)(2,1)S(1)} async-done(((bf16[8,9,2048]{2,1,0:T(8,128)(2,1)}), bf16[8,9,2048]{2,1,0:T(8,128)(2,1)S(1)}, u32[]{:S(2)}, u32[]{:S(2)}) %all-to-all-start) | async-done | bytes 294944 | tf_op jit(solution)/shard_map/while/body/eval_jaxpr/all_to_all | solution.py:121
  212.9 14.1 %conditional.3 = (bf16[72,2048]{1,0:T(8,128)(2,1)S(1)}, bf16[72]{0:T(256)(128)(2,1)S(1)}) conditional(s32[]{:T(128)} %convert_element_type.180, () %tuple.64, (bf16[8,9,2048]{2,1,0:T(8,128)(2,1)S(1)}, bf16[1024,2048]{1,0:T(8,128)(2,1)}, bf16[8,9,2048]{2,1,0:T(8,128)(2,1)S(1)}, bf16[2048,1024]{1,0:T(8,128)(2,1)}, bf16[2048,1024]{1,0:T(8,128)(2,1)}) %tuple.65), branch_computations={%region_6.6_spmd, %region_7.8_spmd} | conditional | flops 1814298624 | bytes 82280696 | solution.py:132
  269.0 13.7 %all-to-all-done.1 = bf16[8,9,2048]{2,1,0:T(8,128)(2,1)S(1)} async-done(((bf16[8,9,2048]{2,1,0:T(8,128)(2,1)}), bf16[8,9,2048]{2,1,0:T(8,128)(2,1)S(1)}, u32[]{:S(2)}, u32[]{:S(2)}) %all-to-all-start.1) | async-done | bytes 294944 | tf_op jit(solution)/shard_map/while/body/eval_jaxpr/all_to_all | solution.py:120
  286.6 14.5 %all-to-all-done = bf16[8,9,2048]{2,1,0:T(8,128)(2,1)S(1)} async-done(((bf16[8,9,2048]{2,1,0:T(8,128)(2,1)}), bf16[8,9,2048]{2,1,0:T(8,128)(2,1)S(1)}, u32[]{:S(2)}, u32[]{:S(2)}) %all-to-all-start) | async-done | bytes 294944 | tf_op jit(solution)/shard_map/while/body/eval_jaxpr/all_to_all | solution.py:121
  301.1 14.1 %conditional.3 = (bf16[72,2048]{1,0:T(8,128)(2,1)S(1)}, bf16[72]{0:T(256)(128)(2,1)S(1)}) conditional(s32[]{:T(128)} %convert_element_type.180, () %tuple.64, (bf16[8,9,2048]{2,1,0:T(8,128)(2,1)S(1)}, bf16[1024,2048]{1,0:T(8,128)(2,1)}, bf16[8,9,2048]{2,1,0:T(8,128)(2,1)S(1)}, bf16[2048,1024]{1,0:T(8,128)(2,1)}, bf16[2048,1024]{1,0:T(8,128)(2,1)}) %tuple.65), branch_computations={%region_6.6_spmd, %region_7.8_spmd} | conditional | flops 1814298624 | bytes 82280696 | solution.py:132
  329.9 13.0 %all-to-all-done.2 = bf16[8,9,2048]{2,1,0:T(8,128)(2,1)S(1)} async-done(((bf16[8,9,2048]{2,1,0:T(8,128)(2,1)}), bf16[8,9,2048]{2,1,0:T(8,128)(2,1)S(1)}, u32[]{:S(2)}, u32[]{:S(2)}) %all-to-all-start.2) | async-done | bytes 294944 | tf_op jit(solution)/shard_map/while/body/eval_jaxpr/all_to_all | solution.py:134
  357.2 13.7 %all-to-all-done.1 = bf16[8,9,2048]{2,1,0:T(8,128)(2,1)S(1)} async-done(((bf16[8,9,2048]{2,1,0:T(8,128)(2,1)}), bf16[8,9,2048]{2,1,0:T(8,128)(2,1)S(1)}, u32[]{:S(2)}, u32[]{:S(2)}) %all-to-all-start.1) | async-done | bytes 294944 | tf_op jit(solution)/shard_map/while/body/eval_jaxpr/all_to_all | solution.py:120
  374.7 14.5 %all-to-all-done = bf16[8,9,2048]{2,1,0:T(8,128)(2,1)S(1)} async-done(((bf16[8,9,2048]{2,1,0:T(8,128)(2,1)}), bf16[8,9,2048]{2,1,0:T(8,128)(2,1)S(1)}, u32[]{:S(2)}, u32[]{:S(2)}) %all-to-all-start) | async-done | bytes 294944 | tf_op jit(solution)/shard_map/while/body/eval_jaxpr/all_to_all | solution.py:121
  389.2 14.1 %conditional.3 = (bf16[72,2048]{1,0:T(8,128)(2,1)S(1)}, bf16[72]{0:T(256)(128)(2,1)S(1)}) conditional(s32[]{:T(128)} %convert_element_type.180, () %tuple.64, (bf16[8,9,2048]{2,1,0:T(8,128)(2,1)S(1)}, bf16[1024,2048]{1,0:T(8,128)(2,1)}, bf16[8,9,2048]{2,1,0:T(8,128)(2,1)S(1)}, bf16[2048,1024]{1,0:T(8,128)(2,1)}, bf16[2048,1024]{1,0:T(8,128)(2,1)}) %tuple.65), branch_computations={%region_6.6_spmd, %region_7.8_spmd} | conditional | flops 1814298624 | bytes 82280696 | solution.py:132
  445.4 13.7 %all-to-all-done.1 = bf16[8,9,2048]{2,1,0:T(8,128)(2,1)S(1)} async-done(((bf16[8,9,2048]{2,1,0:T(8,128)(2,1)}), bf16[8,9,2048]{2,1,0:T(8,128)(2,1)S(1)}, u32[]{:S(2)}, u32[]{:S(2)}) %all-to-all-start.1) | async-done | bytes 294944 | tf_op jit(solution)/shard_map/while/body/eval_jaxpr/all_to_all | solution.py:120
  462.9 14.5 %all-to-all-done = bf16[8,9,2048]{2,1,0:T(8,128)(2,1)S(1)} async-done(((bf16[8,9,2048]{2,1,0:T(8,128)(2,1)}), bf16[8,9,2048]{2,1,0:T(8,128)(2,1)S(1)}, u32[]{:S(2)}, u32[]{:S(2)}) %all-to-all-start) | async-done | bytes 294944 | tf_op jit(solution)/shard_map/while/body/eval_jaxpr/all_to_all | solution.py:121
  477.4 14.1 %conditional.3 = (bf16[72,2048]{1,0:T(8,128)(2,1)S(1)}, bf16[72]{0:T(256)(128)(2,1)S(1)}) conditional(s32[]{:T(128)} %convert_element_type.180, () %tuple.64, (bf16[8,9,2048]{2,1,0:T(8,128)(2,1)S(1)}, bf16[1024,2048]{1,0:T(8,128)(2,1)}, bf16[8,9,2048]{2,1,0:T(8,128)(2,1)S(1)}, bf16[2048,1024]{1,0:T(8,128)(2,1)}, bf16[2048,1024]{1,0:T(8,128)(2,1)}) %tuple.65), branch_computations={%region_6.6_spmd, %region_7.8_spmd} | conditional | flops 1814298624 | bytes 82280696 | solution.py:132
  533.5 13.7 %all-to-all-done.1 = bf16[8,9,2048]{2,1,0:T(8,128)(2,1)S(1)} async-done(((bf16[8,9,2048]{2,1,0:T(8,128)(2,1)}), bf16[8,9,2048]{2,1,0:T(8,128)(2,1)S(1)}, u32[]{:S(2)}, u32[]{:S(2)}) %all-to-all-start.1) | async-done | bytes 294944 | tf_op jit(solution)/shard_map/while/body/eval_jaxpr/all_to_all | solution.py:120
  551.0 14.5 %all-to-all-done = bf16[8,9,2048]{2,1,0:T(8,128)(2,1)S(1)} async-done(((bf16[8,9,2048]{2,1,0:T(8,128)(2,1)}), bf16[8,9,2048]{2,1,0:T(8,128)(2,1)S(1)}, u32[]{:S(2)}, u32[]{:S(2)}) %all-to-all-start) | async-done | bytes 294944 | tf_op jit(solution)/shard_map/while/body/eval_jaxpr/all_to_all | solution.py:121
  565.5 14.1 %conditional.3 = (bf16[72,2048]{1,0:T(8,128)(2,1)S(1)}, bf16[72]{0:T(256)(128)(2,1)S(1)}) conditional(s32[]{:T(128)} %convert_element_type.180, () %tuple.64, (bf16[8,9,2048]{2,1,0:T(8,128)(2,1)S(1)}, bf16[1024,2048]{1,0:T(8,128)(2,1)}, bf16[8,9,2048]{2,1,0:T(8,128)(2,1)S(1)}, bf16[2048,1024]{1,0:T(8,128)(2,1)}, bf16[2048,1024]{1,0:T(8,128)(2,1)}) %tuple.65), branch_computations={%region_6.6_spmd, %region_7.8_spmd} | conditional | flops 1814298624 | bytes 82280696 | solution.py:132
  621.7 13.7 %all-to-all-done.1 = bf16[8,9,2048]{2,1,0:T(8,128)(2,1)S(1)} async-done(((bf16[8,9,2048]{2,1,0:T(8,128)(2,1)}), bf16[8,9,2048]{2,1,0:T(8,128)(2,1)S(1)}, u32[]{:S(2)}, u32[]{:S(2)}) %all-to-all-start.1) | async-done | bytes 294944 | tf_op jit(solution)/shard_map/while/body/eval_jaxpr/all_to_all | solution.py:120
  639.2 14.5 %all-to-all-done = bf16[8,9,2048]{2,1,0:T(8,128)(2,1)S(1)} async-done(((bf16[8,9,2048]{2,1,0:T(8,128)(2,1)}), bf16[8,9,2048]{2,1,0:T(8,128)(2,1)S(1)}, u32[]{:S(2)}, u32[]{:S(2)}) %all-to-all-start) | async-done | bytes 294944 | tf_op jit(solution)/shard_map/while/body/eval_jaxpr/all_to_all | solution.py:121
  653.7 14.1 %conditional.3 = (bf16[72,2048]{1,0:T(8,128)(2,1)S(1)}, bf16[72]{0:T(256)(128)(2,1)S(1)}) conditional(s32[]{:T(128)} %convert_element_type.180, () %tuple.64, (bf16[8,9,2048]{2,1,0:T(8,128)(2,1)S(1)}, bf16[1024,2048]{1,0:T(8,128)(2,1)}, bf16[8,9,2048]{2,1,0:T(8,128)(2,1)S(1)}, bf16[2048,1024]{1,0:T(8,128)(2,1)}, bf16[2048,1024]{1,0:T(8,128)(2,1)}) %tuple.65), branch_computations={%region_6.6_spmd, %region_7.8_spmd} | conditional | flops 1814298624 | bytes 82280696 | solution.py:132
  709.8 13.7 %all-to-all-done.1 = bf16[8,9,2048]{2,1,0:T(8,128)(2,1)S(1)} async-done(((bf16[8,9,2048]{2,1,0:T(8,128)(2,1)}), bf16[8,9,2048]{2,1,0:T(8,128)(2,1)S(1)}, u32[]{:S(2)}, u32[]{:S(2)}) %all-to-all-start.1) | async-done | bytes 294944 | tf_op jit(solution)/shard_map/while/body/eval_jaxpr/all_to_all | solution.py:120
  727.4 14.5 %all-to-all-done = bf16[8,9,2048]{2,1,0:T(8,128)(2,1)S(1)} async-done(((bf16[8,9,2048]{2,1,0:T(8,128)(2,1)}), bf16[8,9,2048]{2,1,0:T(8,128)(2,1)S(1)}, u32[]{:S(2)}, u32[]{:S(2)}) %all-to-all-start) | async-done | bytes 294944 | tf_op jit(solution)/shard_map/while/body/eval_jaxpr/all_to_all | solution.py:121
  741.9 14.1 %conditional.3 = (bf16[72,2048]{1,0:T(8,128)(2,1)S(1)}, bf16[72]{0:T(256)(128)(2,1)S(1)}) conditional(s32[]{:T(128)} %convert_element_type.180, () %tuple.64, (bf16[8,9,2048]{2,1,0:T(8,128)(2,1)S(1)}, bf16[1024,2048]{1,0:T(8,128)(2,1)}, bf16[8,9,2048]{2,1,0:T(8,128)(2,1)S(1)}, bf16[2048,1024]{1,0:T(8,128)(2,1)}, bf16[2048,1024]{1,0:T(8,128)(2,1)}) %tuple.65), branch_computations={%region_6.6_spmd, %region_7.8_spmd} | conditional | flops 1814298624 | bytes 82280696 | solution.py:132
  794.8 13.7 %all-to-all-done.1 = bf16[8,9,2048]{2,1,0:T(8,128)(2,1)S(1)} async-done(((bf16[8,9,2048]{2,1,0:T(8,128)(2,1)}), bf16[8,9,2048]{2,1,0:T(8,128)(2,1)S(1)}, u32[]{:S(2)}, u32[]{:S(2)}) %all-to-all-start.1) | async-done | bytes 294944 | tf_op jit(solution)/shard_map/while/body/eval_jaxpr/all_to_all | solution.py:120
  812.3 14.5 %all-to-all-done = bf16[8,9,2048]{2,1,0:T(8,128)(2,1)S(1)} async-done(((bf16[8,9,2048]{2,1,0:T(8,128)(2,1)}), bf16[8,9,2048]{2,1,0:T(8,128)(2,1)S(1)}, u32[]{:S(2)}, u32[]{:S(2)}) %all-to-all-start) | async-done | bytes 294944 | tf_op jit(solution)/shard_map/while/body/eval_jaxpr/all_to_all | solution.py:121
  841.6 13.0 %all-to-all-done.2 = bf16[8,9,2048]{2,1,0:T(8,128)(2,1)S(1)} async-done(((bf16[8,9,2048]{2,1,0:T(8,128)(2,1)}), bf16[8,9,2048]{2,1,0:T(8,128)(2,1)S(1)}, u32[]{:S(2)}, u32[]{:S(2)}) %all-to-all-start.2) | async-done | bytes 294944 | tf_op jit(solution)/shard_map/while/body/eval_jaxpr/all_to_all | solution.py:134
  868.9 13.7 %all-to-all-done.1 = bf16[8,9,2048]{2,1,0:T(8,128)(2,1)S(1)} async-done(((bf16[8,9,2048]{2,1,0:T(8,128)(2,1)}), bf16[8,9,2048]{2,1,0:T(8,128)(2,1)S(1)}, u32[]{:S(2)}, u32[]{:S(2)}) %all-to-all-start.1) | async-done | bytes 294944 | tf_op jit(solution)/shard_map/while/body/eval_jaxpr/all_to_all | solution.py:120
  886.4 14.5 %all-to-all-done = bf16[8,9,2048]{2,1,0:T(8,128)(2,1)S(1)} async-done(((bf16[8,9,2048]{2,1,0:T(8,128)(2,1)}), bf16[8,9,2048]{2,1,0:T(8,128)(2,1)S(1)}, u32[]{:S(2)}, u32[]{:S(2)}) %all-to-all-start) | async-done | bytes 294944 | tf_op jit(solution)/shard_map/while/body/eval_jaxpr/all_to_all | solution.py:121
  915.6 13.0 %all-to-all-done.2 = bf16[8,9,2048]{2,1,0:T(8,128)(2,1)S(1)} async-done(((bf16[8,9,2048]{2,1,0:T(8,128)(2,1)}), bf16[8,9,2048]{2,1,0:T(8,128)(2,1)S(1)}, u32[]{:S(2)}, u32[]{:S(2)}) %all-to-all-start.2) | async-done | bytes 294944 | tf_op jit(solution)/shard_map/while/body/eval_jaxpr/all_to_all | solution.py:134
  (655 shorter events, 607.4 us)
Async XLA Ops:
  16.6 20.1 %all-to-all-start.1 = ((bf16[8,9,2048]{2,1,0:T(8,128)(2,1)}), bf16[8,9,2048]{2,1,0:T(8,128)(2,1)S(1)}, u32[]{:S(2)}, u32[]{:S(2)}) async-start(bf16[8,9,2048]{2,1,0:T(8,128)(2,1)} %reshape.265), calls=%async_computation.1 | async-start | bytes 1048576 | tf_op jit(solution)/shard_map/while/body/eval_jaxpr/all_to_all | solution.py:120
  36.7 18.2 %all-to-all-start = ((bf16[8,9,2048]{2,1,0:T(8,128)(2,1)}), bf16[8,9,2048]{2,1,0:T(8,128)(2,1)S(1)}, u32[]{:S(2)}, u32[]{:S(2)}) async-start(bf16[8,9,2048]{2,1,0:T(8,128)(2,1)} %reshape.263), calls=%async_computation | async-start | bytes 1048576 | tf_op jit(solution)/shard_map/while/body/eval_jaxpr/all_to_all | solution.py:121
  82.1 13.8 %collective-permute-start = (bf16[16,2048]{1,0:T(8,128)(2,1)S(1)}, bf16[16,2048]{1,0:T(8,128)(2,1)S(1)}, u32[]{:S(2)}, u32[]{:S(2)}) collective-permute-start(bf16[16,2048]{1,0:T(8,128)(2,1)S(1)} %broadcast_select_fusion.2), channel_id=1, source_target_pairs={{8,0},{16,8},{24,16},{9,1},{17,9},{25,17},{10,2},{18,10},{26,18},{... | collective-permute-start | bytes 196616 | tf_op jit(solution)/shard_map/while/body/eval_jaxpr/ppermute | solution.py:10
  91.1 14.7 %all-to-all-start.1 = ((bf16[8,9,2048]{2,1,0:T(8,128)(2,1)}), bf16[8,9,2048]{2,1,0:T(8,128)(2,1)S(1)}, u32[]{:S(2)}, u32[]{:S(2)}) async-start(bf16[8,9,2048]{2,1,0:T(8,128)(2,1)} %reshape.265), calls=%async_computation.1 | async-start | bytes 1048576 | tf_op jit(solution)/shard_map/while/body/eval_jaxpr/all_to_all | solution.py:120
  105.8 14.3 %all-to-all-start = ((bf16[8,9,2048]{2,1,0:T(8,128)(2,1)}), bf16[8,9,2048]{2,1,0:T(8,128)(2,1)S(1)}, u32[]{:S(2)}, u32[]{:S(2)}) async-start(bf16[8,9,2048]{2,1,0:T(8,128)(2,1)} %reshape.263), calls=%async_computation | async-start | bytes 1048576 | tf_op jit(solution)/shard_map/while/body/eval_jaxpr/all_to_all | solution.py:121
  147.4 18.9 %all-to-all-start.2 = ((bf16[8,9,2048]{2,1,0:T(8,128)(2,1)}), bf16[8,9,2048]{2,1,0:T(8,128)(2,1)S(1)}, u32[]{:S(2)}, u32[]{:S(2)}) async-start(bf16[8,9,2048]{2,1,0:T(8,128)(2,1)} %reshape.266), calls=%async_computation.2 | async-start | bytes 1048576 | tf_op jit(solution)/shard_map/while/body/eval_jaxpr/all_to_all | solution.py:134
  175.3 19.2 %all-to-all-start.1 = ((bf16[8,9,2048]{2,1,0:T(8,128)(2,1)}), bf16[8,9,2048]{2,1,0:T(8,128)(2,1)S(1)}, u32[]{:S(2)}, u32[]{:S(2)}) async-start(bf16[8,9,2048]{2,1,0:T(8,128)(2,1)} %reshape.265), calls=%async_computation.1 | async-start | bytes 1048576 | tf_op jit(solution)/shard_map/while/body/eval_jaxpr/all_to_all | solution.py:120
  194.6 18.3 %all-to-all-start = ((bf16[8,9,2048]{2,1,0:T(8,128)(2,1)}), bf16[8,9,2048]{2,1,0:T(8,128)(2,1)S(1)}, u32[]{:S(2)}, u32[]{:S(2)}) async-start(bf16[8,9,2048]{2,1,0:T(8,128)(2,1)} %reshape.263), calls=%async_computation | async-start | bytes 1048576 | tf_op jit(solution)/shard_map/while/body/eval_jaxpr/all_to_all | solution.py:121
  237.9 16.9 %all-to-all-start.2 = ((bf16[8,9,2048]{2,1,0:T(8,128)(2,1)}), bf16[8,9,2048]{2,1,0:T(8,128)(2,1)S(1)}, u32[]{:S(2)}, u32[]{:S(2)}) async-start(bf16[8,9,2048]{2,1,0:T(8,128)(2,1)} %reshape.266), calls=%async_computation.2 | async-start | bytes 1048576 | tf_op jit(solution)/shard_map/while/body/eval_jaxpr/all_to_all | solution.py:134
  263.9 18.8 %all-to-all-start.1 = ((bf16[8,9,2048]{2,1,0:T(8,128)(2,1)}), bf16[8,9,2048]{2,1,0:T(8,128)(2,1)S(1)}, u32[]{:S(2)}, u32[]{:S(2)}) async-start(bf16[8,9,2048]{2,1,0:T(8,128)(2,1)} %reshape.265), calls=%async_computation.1 | async-start | bytes 1048576 | tf_op jit(solution)/shard_map/while/body/eval_jaxpr/all_to_all | solution.py:120
  282.8 18.3 %all-to-all-start = ((bf16[8,9,2048]{2,1,0:T(8,128)(2,1)}), bf16[8,9,2048]{2,1,0:T(8,128)(2,1)S(1)}, u32[]{:S(2)}, u32[]{:S(2)}) async-start(bf16[8,9,2048]{2,1,0:T(8,128)(2,1)} %reshape.263), calls=%async_computation | async-start | bytes 1048576 | tf_op jit(solution)/shard_map/while/body/eval_jaxpr/all_to_all | solution.py:121
  326.0 16.9 %all-to-all-start.2 = ((bf16[8,9,2048]{2,1,0:T(8,128)(2,1)}), bf16[8,9,2048]{2,1,0:T(8,128)(2,1)S(1)}, u32[]{:S(2)}, u32[]{:S(2)}) async-start(bf16[8,9,2048]{2,1,0:T(8,128)(2,1)} %reshape.266), calls=%async_computation.2 | async-start | bytes 1048576 | tf_op jit(solution)/shard_map/while/body/eval_jaxpr/all_to_all | solution.py:134
  352.1 18.8 %all-to-all-start.1 = ((bf16[8,9,2048]{2,1,0:T(8,128)(2,1)}), bf16[8,9,2048]{2,1,0:T(8,128)(2,1)S(1)}, u32[]{:S(2)}, u32[]{:S(2)}) async-start(bf16[8,9,2048]{2,1,0:T(8,128)(2,1)} %reshape.265), calls=%async_computation.1 | async-start | bytes 1048576 | tf_op jit(solution)/shard_map/while/body/eval_jaxpr/all_to_all | solution.py:120
  370.9 18.3 %all-to-all-start = ((bf16[8,9,2048]{2,1,0:T(8,128)(2,1)}), bf16[8,9,2048]{2,1,0:T(8,128)(2,1)S(1)}, u32[]{:S(2)}, u32[]{:S(2)}) async-start(bf16[8,9,2048]{2,1,0:T(8,128)(2,1)} %reshape.263), calls=%async_computation | async-start | bytes 1048576 | tf_op jit(solution)/shard_map/while/body/eval_jaxpr/all_to_all | solution.py:121
  414.2 16.9 %all-to-all-start.2 = ((bf16[8,9,2048]{2,1,0:T(8,128)(2,1)}), bf16[8,9,2048]{2,1,0:T(8,128)(2,1)S(1)}, u32[]{:S(2)}, u32[]{:S(2)}) async-start(bf16[8,9,2048]{2,1,0:T(8,128)(2,1)} %reshape.266), calls=%async_computation.2 | async-start | bytes 1048576 | tf_op jit(solution)/shard_map/while/body/eval_jaxpr/all_to_all | solution.py:134
  440.2 18.8 %all-to-all-start.1 = ((bf16[8,9,2048]{2,1,0:T(8,128)(2,1)}), bf16[8,9,2048]{2,1,0:T(8,128)(2,1)S(1)}, u32[]{:S(2)}, u32[]{:S(2)}) async-start(bf16[8,9,2048]{2,1,0:T(8,128)(2,1)} %reshape.265), calls=%async_computation.1 | async-start | bytes 1048576 | tf_op jit(solution)/shard_map/while/body/eval_jaxpr/all_to_all | solution.py:120
  459.1 18.3 %all-to-all-start = ((bf16[8,9,2048]{2,1,0:T(8,128)(2,1)}), bf16[8,9,2048]{2,1,0:T(8,128)(2,1)S(1)}, u32[]{:S(2)}, u32[]{:S(2)}) async-start(bf16[8,9,2048]{2,1,0:T(8,128)(2,1)} %reshape.263), calls=%async_computation | async-start | bytes 1048576 | tf_op jit(solution)/shard_map/while/body/eval_jaxpr/all_to_all | solution.py:121
  502.3 16.9 %all-to-all-start.2 = ((bf16[8,9,2048]{2,1,0:T(8,128)(2,1)}), bf16[8,9,2048]{2,1,0:T(8,128)(2,1)S(1)}, u32[]{:S(2)}, u32[]{:S(2)}) async-start(bf16[8,9,2048]{2,1,0:T(8,128)(2,1)} %reshape.266), calls=%async_computation.2 | async-start | bytes 1048576 | tf_op jit(solution)/shard_map/while/body/eval_jaxpr/all_to_all | solution.py:134
  528.4 18.8 %all-to-all-start.1 = ((bf16[8,9,2048]{2,1,0:T(8,128)(2,1)}), bf16[8,9,2048]{2,1,0:T(8,128)(2,1)S(1)}, u32[]{:S(2)}, u32[]{:S(2)}) async-start(bf16[8,9,2048]{2,1,0:T(8,128)(2,1)} %reshape.265), calls=%async_computation.1 | async-start | bytes 1048576 | tf_op jit(solution)/shard_map/while/body/eval_jaxpr/all_to_all | solution.py:120
  547.2 18.3 %all-to-all-start = ((bf16[8,9,2048]{2,1,0:T(8,128)(2,1)}), bf16[8,9,2048]{2,1,0:T(8,128)(2,1)S(1)}, u32[]{:S(2)}, u32[]{:S(2)}) async-start(bf16[8,9,2048]{2,1,0:T(8,128)(2,1)} %reshape.263), calls=%async_computation | async-start | bytes 1048576 | tf_op jit(solution)/shard_map/while/body/eval_jaxpr/all_to_all | solution.py:121
  590.5 16.9 %all-to-all-start.2 = ((bf16[8,9,2048]{2,1,0:T(8,128)(2,1)}), bf16[8,9,2048]{2,1,0:T(8,128)(2,1)S(1)}, u32[]{:S(2)}, u32[]{:S(2)}) async-start(bf16[8,9,2048]{2,1,0:T(8,128)(2,1)} %reshape.266), calls=%async_computation.2 | async-start | bytes 1048576 | tf_op jit(solution)/shard_map/while/body/eval_jaxpr/all_to_all | solution.py:134
  616.5 18.8 %all-to-all-start.1 = ((bf16[8,9,2048]{2,1,0:T(8,128)(2,1)}), bf16[8,9,2048]{2,1,0:T(8,128)(2,1)S(1)}, u32[]{:S(2)}, u32[]{:S(2)}) async-start(bf16[8,9,2048]{2,1,0:T(8,128)(2,1)} %reshape.265), calls=%async_computation.1 | async-start | bytes 1048576 | tf_op jit(solution)/shard_map/while/body/eval_jaxpr/all_to_all | solution.py:120
  635.4 18.3 %all-to-all-start = ((bf16[8,9,2048]{2,1,0:T(8,128)(2,1)}), bf16[8,9,2048]{2,1,0:T(8,128)(2,1)S(1)}, u32[]{:S(2)}, u32[]{:S(2)}) async-start(bf16[8,9,2048]{2,1,0:T(8,128)(2,1)} %reshape.263), calls=%async_computation | async-start | bytes 1048576 | tf_op jit(solution)/shard_map/while/body/eval_jaxpr/all_to_all | solution.py:121
  678.7 16.9 %all-to-all-start.2 = ((bf16[8,9,2048]{2,1,0:T(8,128)(2,1)}), bf16[8,9,2048]{2,1,0:T(8,128)(2,1)S(1)}, u32[]{:S(2)}, u32[]{:S(2)}) async-start(bf16[8,9,2048]{2,1,0:T(8,128)(2,1)} %reshape.266), calls=%async_computation.2 | async-start | bytes 1048576 | tf_op jit(solution)/shard_map/while/body/eval_jaxpr/all_to_all | solution.py:134
  704.7 18.8 %all-to-all-start.1 = ((bf16[8,9,2048]{2,1,0:T(8,128)(2,1)}), bf16[8,9,2048]{2,1,0:T(8,128)(2,1)S(1)}, u32[]{:S(2)}, u32[]{:S(2)}) async-start(bf16[8,9,2048]{2,1,0:T(8,128)(2,1)} %reshape.265), calls=%async_computation.1 | async-start | bytes 1048576 | tf_op jit(solution)/shard_map/while/body/eval_jaxpr/all_to_all | solution.py:120
  723.6 18.3 %all-to-all-start = ((bf16[8,9,2048]{2,1,0:T(8,128)(2,1)}), bf16[8,9,2048]{2,1,0:T(8,128)(2,1)S(1)}, u32[]{:S(2)}, u32[]{:S(2)}) async-start(bf16[8,9,2048]{2,1,0:T(8,128)(2,1)} %reshape.263), calls=%async_computation | async-start | bytes 1048576 | tf_op jit(solution)/shard_map/while/body/eval_jaxpr/all_to_all | solution.py:121
  789.6 18.8 %all-to-all-start.1 = ((bf16[8,9,2048]{2,1,0:T(8,128)(2,1)}), bf16[8,9,2048]{2,1,0:T(8,128)(2,1)S(1)}, u32[]{:S(2)}, u32[]{:S(2)}) async-start(bf16[8,9,2048]{2,1,0:T(8,128)(2,1)} %reshape.265), calls=%async_computation.1 | async-start | bytes 1048576 | tf_op jit(solution)/shard_map/while/body/eval_jaxpr/all_to_all | solution.py:120
  808.5 18.3 %all-to-all-start = ((bf16[8,9,2048]{2,1,0:T(8,128)(2,1)}), bf16[8,9,2048]{2,1,0:T(8,128)(2,1)S(1)}, u32[]{:S(2)}, u32[]{:S(2)}) async-start(bf16[8,9,2048]{2,1,0:T(8,128)(2,1)} %reshape.263), calls=%async_computation | async-start | bytes 1048576 | tf_op jit(solution)/shard_map/while/body/eval_jaxpr/all_to_all | solution.py:121
  837.7 16.9 %all-to-all-start.2 = ((bf16[8,9,2048]{2,1,0:T(8,128)(2,1)}), bf16[8,9,2048]{2,1,0:T(8,128)(2,1)S(1)}, u32[]{:S(2)}, u32[]{:S(2)}) async-start(bf16[8,9,2048]{2,1,0:T(8,128)(2,1)} %reshape.266), calls=%async_computation.2 | async-start | bytes 1048576 | tf_op jit(solution)/shard_map/while/body/eval_jaxpr/all_to_all | solution.py:134
  863.7 18.8 %all-to-all-start.1 = ((bf16[8,9,2048]{2,1,0:T(8,128)(2,1)}), bf16[8,9,2048]{2,1,0:T(8,128)(2,1)S(1)}, u32[]{:S(2)}, u32[]{:S(2)}) async-start(bf16[8,9,2048]{2,1,0:T(8,128)(2,1)} %reshape.265), calls=%async_computation.1 | async-start | bytes 1048576 | tf_op jit(solution)/shard_map/while/body/eval_jaxpr/all_to_all | solution.py:120
  882.6 18.3 %all-to-all-start = ((bf16[8,9,2048]{2,1,0:T(8,128)(2,1)}), bf16[8,9,2048]{2,1,0:T(8,128)(2,1)S(1)}, u32[]{:S(2)}, u32[]{:S(2)}) async-start(bf16[8,9,2048]{2,1,0:T(8,128)(2,1)} %reshape.263), calls=%async_computation | async-start | bytes 1048576 | tf_op jit(solution)/shard_map/while/body/eval_jaxpr/all_to_all | solution.py:121
  911.7 16.9 %all-to-all-start.2 = ((bf16[8,9,2048]{2,1,0:T(8,128)(2,1)}), bf16[8,9,2048]{2,1,0:T(8,128)(2,1)S(1)}, u32[]{:S(2)}, u32[]{:S(2)}) async-start(bf16[8,9,2048]{2,1,0:T(8,128)(2,1)} %reshape.266), calls=%async_computation.2 | async-start | bytes 1048576 | tf_op jit(solution)/shard_map/while/body/eval_jaxpr/all_to_all | solution.py:134
  (59 other events, 670.3 us)
where the time goes:
time: 939 us; the launch traced here: 932 us
  waiting for transfers between devices  498 us (53%)
  starting transfers between devices  189 us (20%)
  matrix products  138 us (15%)
  local copies, waits for them, and re-layouts  60.3 us (6%)
  other arithmetic  37.8 us (4%)
    all_to_all x11, waiting for transfers between devices, advance(): lax.all_to_all(sent_grad, 'expert', split_axis=0, concat_axis=0, tiled=True)  155 us
    all_to_all x11, waiting for transfers between devices, advance(): lax.all_to_all(sent_normed, 'expert', split_axis=0, concat_axis=0, tiled=...  144 us
    all_to_all x11, waiting for transfers between devices, advance(): lax.all_to_all(returned.reshape(experts, capacity, width), 'expert', spli...  139 us
    all_to_all x11, waiting for transfers between devices, advance(): lax.all_to_all(dprob.reshape(experts, capacity).astype(jnp.bfloat16), 'ex...  58.5 us
    all_to_all x11, starting transfers between devices, advance(): lax.all_to_all(sent_normed, 'expert', split_axis=0, concat_axis=0, tiled=...  43.6 us
    all_to_all x11, starting transfers between devices, advance(): lax.all_to_all(dprob.reshape(experts, capacity).astype(jnp.bfloat16), 'ex...  42.3 us
    all_to_all x11, starting transfers between devices, advance(): lax.all_to_all(sent_grad, 'expert', split_axis=0, concat_axis=0, tiled=True)  39.9 us
    all_to_all x11, starting transfers between devices, advance(): lax.all_to_all(returned.reshape(experts, capacity, width), 'expert', spli...  38.4 us
  transfers between devices with their start and end apart: 55, of which 45 were waited for; matrix products, arithmetic and copies ran while one was open for 9% of the time, Pallas kernels for 0%

commit v1 on v0

--- a/solution.py
+++ b/solution.py
@@ -1,7 +1,42 @@
+import functools
 import jax
 import jax.numpy as jnp
 from jax import lax
 from jax.sharding import PartitionSpec as P
+
+
+def handle_the_loops(mat, in_dim, page):
+    d_next = mat.shape
+    out_arr = jnp.moveaxis(
+        mat.reshape(*d_next[:in_dim], page, d_next[in_dim] // page, *d_next[in_dim + 1 :]),
+        in_dim,
+        0,
+    )
+    return out_arr
+
+
+def test_object(tile_in, which_dim):
+    kept_arr = list(tile_in.shape[1:])
+    kept_arr[which_dim] *= tile_in.shape[0]
+    long_array = jnp.moveaxis(tile_in, 0, which_dim).reshape(kept_arr)
+    return long_array
+
+
+def replace_the_leaves(point, mesh_dim, unit, my_tile):
+    known, z2 = (jax.lax.psum(1, axis_name=mesh_dim), jax.lax.axis_index(mesh_dim))
+    clean = handle_the_loops(point, unit, known)
+    heap = [clean[z2]]
+    for u in range(1, known):
+        t1 = clean[z2 ^ u]
+        heap.append(
+            jax.lax.ppermute(t1, axis_name=mesh_dim, perm=[(p, p ^ u) for p in range(known)])
+        )
+    clean = jnp.stack(heap, 0)[z2 ^ jnp.arange(known)]
+    next_value = test_object(clean, my_tile)
+    return next_value
+
+
+state_runs = functools.partial(replace_the_leaves, mesh_dim="expert", unit=0, my_tile=0)
 
 
 def shifted(shard, axis, by):
@@ -118,7 +153,7 @@
         sent_grad = pack_rows(select, grad_in, per_token).reshape(experts, capacity, width)
         got_normed, got_grad = (
             lax.all_to_all(sent_normed, "expert", split_axis=0, concat_axis=0, tiled=True),
-            lax.all_to_all(sent_grad, "expert", split_axis=0, concat_axis=0, tiled=True),
+            state_runs(sent_grad),
         )
         rows_normed = got_normed.reshape(slots, width)
         rows_grad = got_grad.reshape(slots, width)

time: 939 us -> 834 us (0.89)
  waiting for transfers between devices: 498 us -> 298 us
  starting transfers between devices: 189 us -> 304 us
  local copies, waits for them, and re-layouts: 60.3 us -> 49.1 us
  matrix products: 138 us -> 127 us
    all_to_all x11 -> x0, waiting for transfers between devices: 155 us -> none  [advance(): lax.all_to_all(sent_grad, 'expert', split_axis=0, concat_axis=0, tiled=True)]
    ppermute x0 -> x77, starting transfers between devices: none -> 152 us  [replace_the_leaves(): jax.lax.ppermute(t1, axis_name=mesh_dim, perm=[(p, p ^ u) for p in range(...]
    all_to_all x11, waiting for transfers between devices: 144 us -> 0.03 us  [advance(): lax.all_to_all(sent_normed, 'expert', split_axis=0, concat_axis=0, tiled=...]
    ppermute x0 -> x77, waiting for transfers between devices: none -> 100 us  [replace_the_leaves(): jax.lax.ppermute(t1, axis_name=mesh_dim, perm=[(p, p ^ u) for p in range(...]
    all_to_all x11 -> x0, starting transfers between devices: 39.9 us -> none  [advance(): lax.all_to_all(sent_grad, 'expert', split_axis=0, concat_axis=0, tiled=True)]
    dot_general x8, matrix products: 28.7 us -> 11.3 us  [expert_rows(): lax.dot_general(grad_rows, down_w, (((1,), (1,)), ((), ())), preferred_el...]
  transfers between devices with their start and end apart: 55 -> 121, of which waited for: 45 -> 44; matrix products, arithmetic and copies ran while one was open for 9% -> 9% of each run, Pallas kernels for 0% -> 0%
where the time goes in v1:
time: 834 us; the launch traced here: 828 us
  starting transfers between devices  304 us (36%)
  waiting for transfers between devices  298 us (36%)
  matrix products  127 us (15%)
  local copies, waits for them, and re-layouts  49.1 us (6%)
  other arithmetic  37.9 us (5%)
    ppermute x77, starting transfers between devices, replace_the_leaves(): jax.lax.ppermute(t1, axis_name=mesh_dim, perm=[(p, p ^ u) for p in range(...  152 us
    all_to_all x11, waiting for transfers between devices, advance(): lax.all_to_all(returned.reshape(experts, capacity, width), 'expert', spli...  139 us
    ppermute x77, waiting for transfers between devices, replace_the_leaves(): jax.lax.ppermute(t1, axis_name=mesh_dim, perm=[(p, p ^ u) for p in range(...  100 us
    all_to_all x11, waiting for transfers between devices, advance(): lax.all_to_all(dprob.reshape(experts, capacity).astype(jnp.bfloat16), 'ex...  58.5 us
    all_to_all x11, starting transfers between devices, advance(): lax.all_to_all(dprob.reshape(experts, capacity).astype(jnp.bfloat16), 'ex...  46.1 us
    all_to_all x11, starting transfers between devices, advance(): lax.all_to_all(sent_normed, 'expert', split_axis=0, concat_axis=0, tiled=...  43.2 us
    all_to_all x11, starting transfers between devices, advance(): lax.all_to_all(returned.reshape(experts, capacity, width), 'expert', spli...  38.4 us
    dot_general x8, matrix products, expert_rows(): gate = jnp.dot(normed_rows, gate_w, preferred_element_type=jnp.float32)  25.6 us
  transfers between devices with their start and end apart: 121, of which 44 were waited for; matrix products, arithmetic and copies ran while one was open for 9% of the time, Pallas kernels for 0%

profile of v1, /device:TPU:2, one launch (start us, length us, event | category | flops | bytes accessed | tf_op | source)
XLA Modules:
  0.0 828.0 jit_solution(6105910699416392118)
XLA Ops:
  1.5 7.0 all_gather.3
  8.6 818.6 %while.18 = (s32[]{:T(128)}, bf16[16,2048]{1,0:T(8,128)(2,1)S(1)}, bf16[8,16,2048]{2,1,0:T(8,128)(2,1)S(1)}, pred[]{:T(512)}, s32[]{:T(128)}, /*index=5*/bf16[8,...) while((s32[]{:T(128)}, bf16[16,2048]{1,0:T(8,128)(2,1)S(1)}, ...), condition=%wide.region_13.14_spmd.clone, body=%wide.region_0.13_spmd.clone.sunk | while | flops 1876002688 | bytes 95948784 | solution.py:208
  37.0 7.0 collective-permute-done.4
  60.5 9.8 %all-to-all-done.1 = bf16[8,9,2048]{2,1,0:T(8,128)(2,1)S(1)} async-done(((bf16[8,9,2048]{2,1,0:T(8,128)(2,1)}), bf16[8,9,2048]{2,1,0:T(8,128)(2,1)S(1)}, u32[]{:S(2)}, u32[]{:S(2)}) %all-to-all-start.1) | async-done | bytes 294944 | tf_op jit(solution)/shard_map/while/body/eval_jaxpr/all_to_all | solution.py:169
  106.4 12.4 %conditional.3 = (bf16[72,2048]{1,0:T(8,128)(2,1)S(1)}, bf16[72]{0:T(256)(128)(2,1)S(1)}) conditional(s32[]{:T(128)} %convert_element_type.185, () %tuple.80, (s32[]{:T(128)}, s32[8,1]{0,1:T(1,128)S(1)}, bf16[8,1,9,2048]{3,2,0,1:T(8,128)(2,1)S(1)}, bf16[1024,2048]{1,0:T(8,128)(2,1)}, bf16[8,9,2048]{2,1,0:T(8,128)(2,1)S(1)}, ...), branch_computations={%region_6.6_spmd, %region_7.8_spmd} | conditional | flops 1814299648 | bytes 82874744 | solution.py:167
  119.4 7.4 all-to-all-start.2
  137.3 14.9 %all-to-all-done.1 = bf16[8,9,2048]{2,1,0:T(8,128)(2,1)S(1)} async-done(((bf16[8,9,2048]{2,1,0:T(8,128)(2,1)}), bf16[8,9,2048]{2,1,0:T(8,128)(2,1)S(1)}, u32[]{:S(2)}, u32[]{:S(2)}) %all-to-all-start.1) | async-done | bytes 294944 | tf_op jit(solution)/shard_map/while/body/eval_jaxpr/all_to_all | solution.py:169
  180.1 7.1 collective-permute-done.4
  189.5 12.4 %conditional.3 = (bf16[72,2048]{1,0:T(8,128)(2,1)S(1)}, bf16[72]{0:T(256)(128)(2,1)S(1)}) conditional(s32[]{:T(128)} %convert_element_type.185, () %tuple.80, (s32[]{:T(128)}, s32[8,1]{0,1:T(1,128)S(1)}, bf16[8,1,9,2048]{3,2,0,1:T(8,128)(2,1)S(1)}, bf16[1024,2048]{1,0:T(8,128)(2,1)}, bf16[8,9,2048]{2,1,0:T(8,128)(2,1)S(1)}, ...), branch_computations={%region_6.6_spmd, %region_7.8_spmd} | conditional | flops 1814299648 | bytes 82874744 | solution.py:167
  216.9 13.0 %all-to-all-done.1 = bf16[8,9,2048]{2,1,0:T(8,128)(2,1)S(1)} async-done(((bf16[8,9,2048]{2,1,0:T(8,128)(2,1)}), bf16[8,9,2048]{2,1,0:T(8,128)(2,1)S(1)}, u32[]{:S(2)}, u32[]{:S(2)}) %all-to-all-start.1) | async-done | bytes 294944 | tf_op jit(solution)/shard_map/while/body/eval_jaxpr/all_to_all | solution.py:169
  257.9 7.1 collective-permute-done.4
  267.4 12.4 %conditional.3 = (bf16[72,2048]{1,0:T(8,128)(2,1)S(1)}, bf16[72]{0:T(256)(128)(2,1)S(1)}) conditional(s32[]{:T(128)} %convert_element_type.185, () %tuple.80, (s32[]{:T(128)}, s32[8,1]{0,1:T(1,128)S(1)}, bf16[8,1,9,2048]{3,2,0,1:T(8,128)(2,1)S(1)}, bf16[1024,2048]{1,0:T(8,128)(2,1)}, bf16[8,9,2048]{2,1,0:T(8,128)(2,1)S(1)}, ...), branch_computations={%region_6.6_spmd, %region_7.8_spmd} | conditional | flops 1814299648 | bytes 82874744 | solution.py:167
  294.8 13.0 %all-to-all-done.1 = bf16[8,9,2048]{2,1,0:T(8,128)(2,1)S(1)} async-done(((bf16[8,9,2048]{2,1,0:T(8,128)(2,1)}), bf16[8,9,2048]{2,1,0:T(8,128)(2,1)S(1)}, u32[]{:S(2)}, u32[]{:S(2)}) %all-to-all-start.1) | async-done | bytes 294944 | tf_op jit(solution)/shard_map/while/body/eval_jaxpr/all_to_all | solution.py:169
  335.7 7.1 collective-permute-done.4
  345.2 12.4 %conditional.3 = (bf16[72,2048]{1,0:T(8,128)(2,1)S(1)}, bf16[72]{0:T(256)(128)(2,1)S(1)}) conditional(s32[]{:T(128)} %convert_element_type.185, () %tuple.80, (s32[]{:T(128)}, s32[8,1]{0,1:T(1,128)S(1)}, bf16[8,1,9,2048]{3,2,0,1:T(8,128)(2,1)S(1)}, bf16[1024,2048]{1,0:T(8,128)(2,1)}, bf16[8,9,2048]{2,1,0:T(8,128)(2,1)S(1)}, ...), branch_computations={%region_6.6_spmd, %region_7.8_spmd} | conditional | flops 1814299648 | bytes 82874744 | solution.py:167
  372.6 13.0 %all-to-all-done.1 = bf16[8,9,2048]{2,1,0:T(8,128)(2,1)S(1)} async-done(((bf16[8,9,2048]{2,1,0:T(8,128)(2,1)}), bf16[8,9,2048]{2,1,0:T(8,128)(2,1)S(1)}, u32[]{:S(2)}, u32[]{:S(2)}) %all-to-all-start.1) | async-done | bytes 294944 | tf_op jit(solution)/shard_map/while/body/eval_jaxpr/all_to_all | solution.py:169
  413.6 7.1 collective-permute-done.4
  423.0 12.4 %conditional.3 = (bf16[72,2048]{1,0:T(8,128)(2,1)S(1)}, bf16[72]{0:T(256)(128)(2,1)S(1)}) conditional(s32[]{:T(128)} %convert_element_type.185, () %tuple.80, (s32[]{:T(128)}, s32[8,1]{0,1:T(1,128)S(1)}, bf16[8,1,9,2048]{3,2,0,1:T(8,128)(2,1)S(1)}, bf16[1024,2048]{1,0:T(8,128)(2,1)}, bf16[8,9,2048]{2,1,0:T(8,128)(2,1)S(1)}, ...), branch_computations={%region_6.6_spmd, %region_7.8_spmd} | conditional | flops 1814299648 | bytes 82874744 | solution.py:167
  450.4 13.0 %all-to-all-done.1 = bf16[8,9,2048]{2,1,0:T(8,128)(2,1)S(1)} async-done(((bf16[8,9,2048]{2,1,0:T(8,128)(2,1)}), bf16[8,9,2048]{2,1,0:T(8,128)(2,1)S(1)}, u32[]{:S(2)}, u32[]{:S(2)}) %all-to-all-start.1) | async-done | bytes 294944 | tf_op jit(solution)/shard_map/while/body/eval_jaxpr/all_to_all | solution.py:169
  491.4 7.1 collective-permute-done.4
  500.8 12.4 %conditional.3 = (bf16[72,2048]{1,0:T(8,128)(2,1)S(1)}, bf16[72]{0:T(256)(128)(2,1)S(1)}) conditional(s32[]{:T(128)} %convert_element_type.185, () %tuple.80, (s32[]{:T(128)}, s32[8,1]{0,1:T(1,128)S(1)}, bf16[8,1,9,2048]{3,2,0,1:T(8,128)(2,1)S(1)}, bf16[1024,2048]{1,0:T(8,128)(2,1)}, bf16[8,9,2048]{2,1,0:T(8,128)(2,1)S(1)}, ...), branch_computations={%region_6.6_spmd, %region_7.8_spmd} | conditional | flops 1814299648 | bytes 82874744 | solution.py:167
  528.2 13.0 %all-to-all-done.1 = bf16[8,9,2048]{2,1,0:T(8,128)(2,1)S(1)} async-done(((bf16[8,9,2048]{2,1,0:T(8,128)(2,1)}), bf16[8,9,2048]{2,1,0:T(8,128)(2,1)S(1)}, u32[]{:S(2)}, u32[]{:S(2)}) %all-to-all-start.1) | async-done | bytes 294944 | tf_op jit(solution)/shard_map/while/body/eval_jaxpr/all_to_all | solution.py:169
  569.2 7.1 collective-permute-done.4
  578.6 12.4 %conditional.3 = (bf16[72,2048]{1,0:T(8,128)(2,1)S(1)}, bf16[72]{0:T(256)(128)(2,1)S(1)}) conditional(s32[]{:T(128)} %convert_element_type.185, () %tuple.80, (s32[]{:T(128)}, s32[8,1]{0,1:T(1,128)S(1)}, bf16[8,1,9,2048]{3,2,0,1:T(8,128)(2,1)S(1)}, bf16[1024,2048]{1,0:T(8,128)(2,1)}, bf16[8,9,2048]{2,1,0:T(8,128)(2,1)S(1)}, ...), branch_computations={%region_6.6_spmd, %region_7.8_spmd} | conditional | flops 1814299648 | bytes 82874744 | solution.py:167
  606.0 13.0 %all-to-all-done.1 = bf16[8,9,2048]{2,1,0:T(8,128)(2,1)S(1)} async-done(((bf16[8,9,2048]{2,1,0:T(8,128)(2,1)}), bf16[8,9,2048]{2,1,0:T(8,128)(2,1)S(1)}, u32[]{:S(2)}, u32[]{:S(2)}) %all-to-all-start.1) | async-done | bytes 294944 | tf_op jit(solution)/shard_map/while/body/eval_jaxpr/all_to_all | solution.py:169
  647.0 7.1 collective-permute-done.4
  656.5 12.4 %conditional.3 = (bf16[72,2048]{1,0:T(8,128)(2,1)S(1)}, bf16[72]{0:T(256)(128)(2,1)S(1)}) conditional(s32[]{:T(128)} %convert_element_type.185, () %tuple.80, (s32[]{:T(128)}, s32[8,1]{0,1:T(1,128)S(1)}, bf16[8,1,9,2048]{3,2,0,1:T(8,128)(2,1)S(1)}, bf16[1024,2048]{1,0:T(8,128)(2,1)}, bf16[8,9,2048]{2,1,0:T(8,128)(2,1)S(1)}, ...), branch_computations={%region_6.6_spmd, %region_7.8_spmd} | conditional | flops 1814299648 | bytes 82874744 | solution.py:167
  683.9 9.8 %all-to-all-done.1 = bf16[8,9,2048]{2,1,0:T(8,128)(2,1)S(1)} async-done(((bf16[8,9,2048]{2,1,0:T(8,128)(2,1)}), bf16[8,9,2048]{2,1,0:T(8,128)(2,1)S(1)}, u32[]{:S(2)}, u32[]{:S(2)}) %all-to-all-start.1) | async-done | bytes 294944 | tf_op jit(solution)/shard_map/while/body/eval_jaxpr/all_to_all | solution.py:169
  721.6 7.1 collective-permute-done.4
  746.1 13.0 %all-to-all-done.1 = bf16[8,9,2048]{2,1,0:T(8,128)(2,1)S(1)} async-done(((bf16[8,9,2048]{2,1,0:T(8,128)(2,1)}), bf16[8,9,2048]{2,1,0:T(8,128)(2,1)S(1)}, u32[]{:S(2)}, u32[]{:S(2)}) %all-to-all-start.1) | async-done | bytes 294944 | tf_op jit(solution)/shard_map/while/body/eval_jaxpr/all_to_all | solution.py:169
  787.1 7.1 collective-permute-done.4
  811.6 13.0 %all-to-all-done.1 = bf16[8,9,2048]{2,1,0:T(8,128)(2,1)S(1)} async-done(((bf16[8,9,2048]{2,1,0:T(8,128)(2,1)}), bf16[8,9,2048]{2,1,0:T(8,128)(2,1)S(1)}, u32[]{:S(2)}, u32[]{:S(2)}) %all-to-all-start.1) | async-done | bytes 294944 | tf_op jit(solution)/shard_map/while/body/eval_jaxpr/all_to_all | solution.py:169
  (910 shorter events, 600.2 us)
Async XLA Ops:
  15.3 30.5 %all-to-all-start = ((bf16[8,9,2048]{2,1,0:T(8,128)(2,1)}), bf16[8,9,2048]{2,1,0:T(8,128)(2,1)S(1)}, u32[]{:S(2)}, u32[]{:S(2)}) async-start(bf16[8,9,2048]{2,1,0:T(8,128)(2,1)} %reshape.281), calls=%async_computation | async-start | bytes 1048576 | tf_op jit(solution)/shard_map/while/body/eval_jaxpr/all_to_all | solution.py:155
  26.5 17.5 %collective-permute-start.4 = (bf16[1,9,2048]{2,1,0:T(8,128)(2,1)S(1)}, bf16[1,9,2048]{2,1,0:T(8,128)(2,1)S(1)}, u32[]{:S(2)}, u32[]{:S(2)}) collective-permute-start(bf16[1,9,2048]{2,1,0:T(8,128)(2,1)S(1)} %get-tuple-element.569), channel_id=1, source_target_pairs={{0,4},{1,5},{2,6},{3,7},{4,0},{5,1},{6,2},{7,3},{8,12},{9,13},{10,... | collective-permute-start | bytes 110600 | tf_op jit(solution)/shard_map/while/body/eval_jaxpr/ppermute | solution.py:32
  81.1 25.2 %all-to-all-start = ((bf16[8,9,2048]{2,1,0:T(8,128)(2,1)}), bf16[8,9,2048]{2,1,0:T(8,128)(2,1)S(1)}, u32[]{:S(2)}, u32[]{:S(2)}) async-start(bf16[8,9,2048]{2,1,0:T(8,128)(2,1)} %reshape.281), calls=%async_computation | async-start | bytes 1048576 | tf_op jit(solution)/shard_map/while/body/eval_jaxpr/all_to_all | solution.py:155
  133.3 18.8 %all-to-all-start.1 = ((bf16[8,9,2048]{2,1,0:T(8,128)(2,1)}), bf16[8,9,2048]{2,1,0:T(8,128)(2,1)S(1)}, u32[]{:S(2)}, u32[]{:S(2)}) async-start(bf16[8,9,2048]{2,1,0:T(8,128)(2,1)} %reshape.282), calls=%async_computation.1 | async-start | bytes 1048576 | tf_op jit(solution)/shard_map/while/body/eval_jaxpr/all_to_all | solution.py:169
  160.6 28.9 %all-to-all-start = ((bf16[8,9,2048]{2,1,0:T(8,128)(2,1)}), bf16[8,9,2048]{2,1,0:T(8,128)(2,1)S(1)}, u32[]{:S(2)}, u32[]{:S(2)}) async-start(bf16[8,9,2048]{2,1,0:T(8,128)(2,1)} %reshape.281), calls=%async_computation | async-start | bytes 1048576 | tf_op jit(solution)/shard_map/while/body/eval_jaxpr/all_to_all | solution.py:155
  169.6 17.5 %collective-permute-start.4 = (bf16[1,9,2048]{2,1,0:T(8,128)(2,1)S(1)}, bf16[1,9,2048]{2,1,0:T(8,128)(2,1)S(1)}, u32[]{:S(2)}, u32[]{:S(2)}) collective-permute-start(bf16[1,9,2048]{2,1,0:T(8,128)(2,1)S(1)} %get-tuple-element.569), channel_id=1, source_target_pairs={{0,4},{1,5},{2,6},{3,7},{4,0},{5,1},{6,2},{7,3},{8,12},{9,13},{10,... | collective-permute-start | bytes 110600 | tf_op jit(solution)/shard_map/while/body/eval_jaxpr/ppermute | solution.py:32
  172.4 17.0 %collective-permute-start.5 = (bf16[1,9,2048]{2,1,0:T(8,128)(2,1)S(1)}, bf16[1,9,2048]{2,1,0:T(8,128)(2,1)S(1)}, u32[]{:S(2)}, u32[]{:S(2)}) collective-permute-start(bf16[1,9,2048]{2,1,0:T(8,128)(2,1)S(1)} %get-tuple-element.570), channel_id=1, source_target_pairs={{0,5},{1,4},{2,7},{3,6},{4,1},{5,0},{6,3},{7,2},{8,13},{9,12},{10,... | collective-permute-start | bytes 110600 | tf_op jit(solution)/shard_map/while/body/eval_jaxpr/ppermute | solution.py:32
  213.0 16.9 %all-to-all-start.1 = ((bf16[8,9,2048]{2,1,0:T(8,128)(2,1)}), bf16[8,9,2048]{2,1,0:T(8,128)(2,1)S(1)}, u32[]{:S(2)}, u32[]{:S(2)}) async-start(bf16[8,9,2048]{2,1,0:T(8,128)(2,1)} %reshape.282), calls=%async_computation.1 | async-start | bytes 1048576 | tf_op jit(solution)/shard_map/while/body/eval_jaxpr/all_to_all | solution.py:169
  238.4 28.9 %all-to-all-start = ((bf16[8,9,2048]{2,1,0:T(8,128)(2,1)}), bf16[8,9,2048]{2,1,0:T(8,128)(2,1)S(1)}, u32[]{:S(2)}, u32[]{:S(2)}) async-start(bf16[8,9,2048]{2,1,0:T(8,128)(2,1)} %reshape.281), calls=%async_computation | async-start | bytes 1048576 | tf_op jit(solution)/shard_map/while/body/eval_jaxpr/all_to_all | solution.py:155
  247.4 17.5 %collective-permute-start.4 = (bf16[1,9,2048]{2,1,0:T(8,128)(2,1)S(1)}, bf16[1,9,2048]{2,1,0:T(8,128)(2,1)S(1)}, u32[]{:S(2)}, u32[]{:S(2)}) collective-permute-start(bf16[1,9,2048]{2,1,0:T(8,128)(2,1)S(1)} %get-tuple-element.569), channel_id=1, source_target_pairs={{0,4},{1,5},{2,6},{3,7},{4,0},{5,1},{6,2},{7,3},{8,12},{9,13},{10,... | collective-permute-start | bytes 110600 | tf_op jit(solution)/shard_map/while/body/eval_jaxpr/ppermute | solution.py:32
  250.3 17.0 %collective-permute-start.5 = (bf16[1,9,2048]{2,1,0:T(8,128)(2,1)S(1)}, bf16[1,9,2048]{2,1,0:T(8,128)(2,1)S(1)}, u32[]{:S(2)}, u32[]{:S(2)}) collective-permute-start(bf16[1,9,2048]{2,1,0:T(8,128)(2,1)S(1)} %get-tuple-element.570), channel_id=1, source_target_pairs={{0,5},{1,4},{2,7},{3,6},{4,1},{5,0},{6,3},{7,2},{8,13},{9,12},{10,... | collective-permute-start | bytes 110600 | tf_op jit(solution)/shard_map/while/body/eval_jaxpr/ppermute | solution.py:32
  316.2 28.9 %all-to-all-start = ((bf16[8,9,2048]{2,1,0:T(8,128)(2,1)}), bf16[8,9,2048]{2,1,0:T(8,128)(2,1)S(1)}, u32[]{:S(2)}, u32[]{:S(2)}) async-start(bf16[8,9,2048]{2,1,0:T(8,128)(2,1)} %reshape.281), calls=%async_computation | async-start | bytes 1048576 | tf_op jit(solution)/shard_map/while/body/eval_jaxpr/all_to_all | solution.py:155
  325.3 17.5 %collective-permute-start.4 = (bf16[1,9,2048]{2,1,0:T(8,128)(2,1)S(1)}, bf16[1,9,2048]{2,1,0:T(8,128)(2,1)S(1)}, u32[]{:S(2)}, u32[]{:S(2)}) collective-permute-start(bf16[1,9,2048]{2,1,0:T(8,128)(2,1)S(1)} %get-tuple-element.569), channel_id=1, source_target_pairs={{0,4},{1,5},{2,6},{3,7},{4,0},{5,1},{6,2},{7,3},{8,12},{9,13},{10,... | collective-permute-start | bytes 110600 | tf_op jit(solution)/shard_map/while/body/eval_jaxpr/ppermute | solution.py:32
  328.1 17.0 %collective-permute-start.5 = (bf16[1,9,2048]{2,1,0:T(8,128)(2,1)S(1)}, bf16[1,9,2048]{2,1,0:T(8,128)(2,1)S(1)}, u32[]{:S(2)}, u32[]{:S(2)}) collective-permute-start(bf16[1,9,2048]{2,1,0:T(8,128)(2,1)S(1)} %get-tuple-element.570), channel_id=1, source_target_pairs={{0,5},{1,4},{2,7},{3,6},{4,1},{5,0},{6,3},{7,2},{8,13},{9,12},{10,... | collective-permute-start | bytes 110600 | tf_op jit(solution)/shard_map/while/body/eval_jaxpr/ppermute | solution.py:32
  394.0 28.9 %all-to-all-start = ((bf16[8,9,2048]{2,1,0:T(8,128)(2,1)}), bf16[8,9,2048]{2,1,0:T(8,128)(2,1)S(1)}, u32[]{:S(2)}, u32[]{:S(2)}) async-start(bf16[8,9,2048]{2,1,0:T(8,128)(2,1)} %reshape.281), calls=%async_computation | async-start | bytes 1048576 | tf_op jit(solution)/shard_map/while/body/eval_jaxpr/all_to_all | solution.py:155
  403.1 17.5 %collective-permute-start.4 = (bf16[1,9,2048]{2,1,0:T(8,128)(2,1)S(1)}, bf16[1,9,2048]{2,1,0:T(8,128)(2,1)S(1)}, u32[]{:S(2)}, u32[]{:S(2)}) collective-permute-start(bf16[1,9,2048]{2,1,0:T(8,128)(2,1)S(1)} %get-tuple-element.569), channel_id=1, source_target_pairs={{0,4},{1,5},{2,6},{3,7},{4,0},{5,1},{6,2},{7,3},{8,12},{9,13},{10,... | collective-permute-start | bytes 110600 | tf_op jit(solution)/shard_map/while/body/eval_jaxpr/ppermute | solution.py:32
  405.9 17.0 %collective-permute-start.5 = (bf16[1,9,2048]{2,1,0:T(8,128)(2,1)S(1)}, bf16[1,9,2048]{2,1,0:T(8,128)(2,1)S(1)}, u32[]{:S(2)}, u32[]{:S(2)}) collective-permute-start(bf16[1,9,2048]{2,1,0:T(8,128)(2,1)S(1)} %get-tuple-element.570), channel_id=1, source_target_pairs={{0,5},{1,4},{2,7},{3,6},{4,1},{5,0},{6,3},{7,2},{8,13},{9,12},{10,... | collective-permute-start | bytes 110600 | tf_op jit(solution)/shard_map/while/body/eval_jaxpr/ppermute | solution.py:32
  471.9 28.9 %all-to-all-start = ((bf16[8,9,2048]{2,1,0:T(8,128)(2,1)}), bf16[8,9,2048]{2,1,0:T(8,128)(2,1)S(1)}, u32[]{:S(2)}, u32[]{:S(2)}) async-start(bf16[8,9,2048]{2,1,0:T(8,128)(2,1)} %reshape.281), calls=%async_computation | async-start | bytes 1048576 | tf_op jit(solution)/shard_map/while/body/eval_jaxpr/all_to_all | solution.py:155
  480.9 17.5 %collective-permute-start.4 = (bf16[1,9,2048]{2,1,0:T(8,128)(2,1)S(1)}, bf16[1,9,2048]{2,1,0:T(8,128)(2,1)S(1)}, u32[]{:S(2)}, u32[]{:S(2)}) collective-permute-start(bf16[1,9,2048]{2,1,0:T(8,128)(2,1)S(1)} %get-tuple-element.569), channel_id=1, source_target_pairs={{0,4},{1,5},{2,6},{3,7},{4,0},{5,1},{6,2},{7,3},{8,12},{9,13},{10,... | collective-permute-start | bytes 110600 | tf_op jit(solution)/shard_map/while/body/eval_jaxpr/ppermute | solution.py:32
  483.7 17.0 %collective-permute-start.5 = (bf16[1,9,2048]{2,1,0:T(8,128)(2,1)S(1)}, bf16[1,9,2048]{2,1,0:T(8,128)(2,1)S(1)}, u32[]{:S(2)}, u32[]{:S(2)}) collective-permute-start(bf16[1,9,2048]{2,1,0:T(8,128)(2,1)S(1)} %get-tuple-element.570), channel_id=1, source_target_pairs={{0,5},{1,4},{2,7},{3,6},{4,1},{5,0},{6,3},{7,2},{8,13},{9,12},{10,... | collective-permute-start | bytes 110600 | tf_op jit(solution)/shard_map/while/body/eval_jaxpr/ppermute | solution.py:32
  549.7 28.9 %all-to-all-start = ((bf16[8,9,2048]{2,1,0:T(8,128)(2,1)}), bf16[8,9,2048]{2,1,0:T(8,128)(2,1)S(1)}, u32[]{:S(2)}, u32[]{:S(2)}) async-start(bf16[8,9,2048]{2,1,0:T(8,128)(2,1)} %reshape.281), calls=%async_computation | async-start | bytes 1048576 | tf_op jit(solution)/shard_map/while/body/eval_jaxpr/all_to_all | solution.py:155
  558.7 17.5 %collective-permute-start.4 = (bf16[1,9,2048]{2,1,0:T(8,128)(2,1)S(1)}, bf16[1,9,2048]{2,1,0:T(8,128)(2,1)S(1)}, u32[]{:S(2)}, u32[]{:S(2)}) collective-permute-start(bf16[1,9,2048]{2,1,0:T(8,128)(2,1)S(1)} %get-tuple-element.569), channel_id=1, source_target_pairs={{0,4},{1,5},{2,6},{3,7},{4,0},{5,1},{6,2},{7,3},{8,12},{9,13},{10,... | collective-permute-start | bytes 110600 | tf_op jit(solution)/shard_map/while/body/eval_jaxpr/ppermute | solution.py:32
  561.6 17.0 %collective-permute-start.5 = (bf16[1,9,2048]{2,1,0:T(8,128)(2,1)S(1)}, bf16[1,9,2048]{2,1,0:T(8,128)(2,1)S(1)}, u32[]{:S(2)}, u32[]{:S(2)}) collective-permute-start(bf16[1,9,2048]{2,1,0:T(8,128)(2,1)S(1)} %get-tuple-element.570), channel_id=1, source_target_pairs={{0,5},{1,4},{2,7},{3,6},{4,1},{5,0},{6,3},{7,2},{8,13},{9,12},{10,... | collective-permute-start | bytes 110600 | tf_op jit(solution)/shard_map/while/body/eval_jaxpr/ppermute | solution.py:32
  627.5 28.9 %all-to-all-start = ((bf16[8,9,2048]{2,1,0:T(8,128)(2,1)}), bf16[8,9,2048]{2,1,0:T(8,128)(2,1)S(1)}, u32[]{:S(2)}, u32[]{:S(2)}) async-start(bf16[8,9,2048]{2,1,0:T(8,128)(2,1)} %reshape.281), calls=%async_computation | async-start | bytes 1048576 | tf_op jit(solution)/shard_map/while/body/eval_jaxpr/all_to_all | solution.py:155
  636.5 17.5 %collective-permute-start.4 = (bf16[1,9,2048]{2,1,0:T(8,128)(2,1)S(1)}, bf16[1,9,2048]{2,1,0:T(8,128)(2,1)S(1)}, u32[]{:S(2)}, u32[]{:S(2)}) collective-permute-start(bf16[1,9,2048]{2,1,0:T(8,128)(2,1)S(1)} %get-tuple-element.569), channel_id=1, source_target_pairs={{0,4},{1,5},{2,6},{3,7},{4,0},{5,1},{6,2},{7,3},{8,12},{9,13},{10,... | collective-permute-start | bytes 110600 | tf_op jit(solution)/shard_map/while/body/eval_jaxpr/ppermute | solution.py:32
  639.4 17.0 %collective-permute-start.5 = (bf16[1,9,2048]{2,1,0:T(8,128)(2,1)S(1)}, bf16[1,9,2048]{2,1,0:T(8,128)(2,1)S(1)}, u32[]{:S(2)}, u32[]{:S(2)}) collective-permute-start(bf16[1,9,2048]{2,1,0:T(8,128)(2,1)S(1)} %get-tuple-element.570), channel_id=1, source_target_pairs={{0,5},{1,4},{2,7},{3,6},{4,1},{5,0},{6,3},{7,2},{8,13},{9,12},{10,... | collective-permute-start | bytes 110600 | tf_op jit(solution)/shard_map/while/body/eval_jaxpr/ppermute | solution.py:32
  702.1 28.9 %all-to-all-start = ((bf16[8,9,2048]{2,1,0:T(8,128)(2,1)}), bf16[8,9,2048]{2,1,0:T(8,128)(2,1)S(1)}, u32[]{:S(2)}, u32[]{:S(2)}) async-start(bf16[8,9,2048]{2,1,0:T(8,128)(2,1)} %reshape.281), calls=%async_computation | async-start | bytes 1048576 | tf_op jit(solution)/shard_map/while/body/eval_jaxpr/all_to_all | solution.py:155
  711.1 17.5 %collective-permute-start.4 = (bf16[1,9,2048]{2,1,0:T(8,128)(2,1)S(1)}, bf16[1,9,2048]{2,1,0:T(8,128)(2,1)S(1)}, u32[]{:S(2)}, u32[]{:S(2)}) collective-permute-start(bf16[1,9,2048]{2,1,0:T(8,128)(2,1)S(1)} %get-tuple-element.569), channel_id=1, source_target_pairs={{0,4},{1,5},{2,6},{3,7},{4,0},{5,1},{6,2},{7,3},{8,12},{9,13},{10,... | collective-permute-start | bytes 110600 | tf_op jit(solution)/shard_map/while/body/eval_jaxpr/ppermute | solution.py:32
  714.0 17.0 %collective-permute-start.5 = (bf16[1,9,2048]{2,1,0:T(8,128)(2,1)S(1)}, bf16[1,9,2048]{2,1,0:T(8,128)(2,1)S(1)}, u32[]{:S(2)}, u32[]{:S(2)}) collective-permute-start(bf16[1,9,2048]{2,1,0:T(8,128)(2,1)S(1)} %get-tuple-element.570), channel_id=1, source_target_pairs={{0,5},{1,4},{2,7},{3,6},{4,1},{5,0},{6,3},{7,2},{8,13},{9,12},{10,... | collective-permute-start | bytes 110600 | tf_op jit(solution)/shard_map/while/body/eval_jaxpr/ppermute | solution.py:32
  767.6 28.9 %all-to-all-start = ((bf16[8,9,2048]{2,1,0:T(8,128)(2,1)}), bf16[8,9,2048]{2,1,0:T(8,128)(2,1)S(1)}, u32[]{:S(2)}, u32[]{:S(2)}) async-start(bf16[8,9,2048]{2,1,0:T(8,128)(2,1)} %reshape.281), calls=%async_computation | async-start | bytes 1048576 | tf_op jit(solution)/shard_map/while/body/eval_jaxpr/all_to_all | solution.py:155
  776.6 17.5 %collective-permute-start.4 = (bf16[1,9,2048]{2,1,0:T(8,128)(2,1)S(1)}, bf16[1,9,2048]{2,1,0:T(8,128)(2,1)S(1)}, u32[]{:S(2)}, u32[]{:S(2)}) collective-permute-start(bf16[1,9,2048]{2,1,0:T(8,128)(2,1)S(1)} %get-tuple-element.569), channel_id=1, source_target_pairs={{0,4},{1,5},{2,6},{3,7},{4,0},{5,1},{6,2},{7,3},{8,12},{9,13},{10,... | collective-permute-start | bytes 110600 | tf_op jit(solution)/shard_map/while/body/eval_jaxpr/ppermute | solution.py:32
  779.4 17.0 %collective-permute-start.5 = (bf16[1,9,2048]{2,1,0:T(8,128)(2,1)S(1)}, bf16[1,9,2048]{2,1,0:T(8,128)(2,1)S(1)}, u32[]{:S(2)}, u32[]{:S(2)}) collective-permute-start(bf16[1,9,2048]{2,1,0:T(8,128)(2,1)S(1)} %get-tuple-element.570), channel_id=1, source_target_pairs={{0,5},{1,4},{2,7},{3,6},{4,1},{5,0},{6,3},{7,2},{8,13},{9,12},{10,... | collective-permute-start | bytes 110600 | tf_op jit(solution)/shard_map/while/body/eval_jaxpr/ppermute | solution.py:32
  (125 other events, 1519.2 us)
